TPU v7x, 32 devices: a whole 2x2x4 slice. The times are simulated.
32 devices in a mesh: lon: 4 (over x, core), lat: 8 (over z, y).
Axes of the slice: x: 2, y: 2, z: 4, core: 2. Of those that a mesh axis runs over, the one named last changes fastest.
Arguments:
- prognostic: float32 [4, 16, 192, 1536], P(None, None, 'lat', 'lon'), may hold values from -6 to 6
- tracers: float32 [4, 16, 192, 1536], P(None, None, 'lat', 'lon'), may hold values from -6 to 6
- zonal_courant: float32 [16, 192, 1536], P(None, 'lat', 'lon'), may hold values from -0.45 to 0.45
- meridional_courant: float32 [16, 192, 1536], P(None, 'lat', 'lon'), may hold values from -0.45 to 0.45
- filter_band: int32 [192], P('lat'), may hold values from 96 to 768, as said below
- dep_owner: int32 [192, 2], P('lat'), may hold values from 0 to 7, as said below
- dep_row: int32 [192, 2], P('lat'), may hold values from 0 to 23
- dep_weight: float32 [192, 2], P('lat'), may hold values from 0 to 1, as said below
Outputs:
- new_prognostic: float32 [4, 16, 192, 1536], P(None, None, 'lat', 'lon')
- new_tracers: float32 [4, 16, 192, 1536], P(None, None, 'lat', 'lon')
Inputs may be any that keep to these rules, and one draw needn't show every extreme that they name: `filter_band`: rows within 24 of either pole hold values below 768; all other rows hold 768. `dep_owner`: among the 48 entries of one band, at most 12 name the same owner band, and some owner is named exactly 12 times; the owners a band names are the bands nearest to it, distance counted across either pole. `dep_weight`: Positive; the 2 weights of a row sum to 1.
All inputs are finite; a program needn't handle non-finite values.
Results may differ from a plain program's by a relative error of at most 0.00007.
Values sent between devices are 32-bit elements; how exact they have to be, the bound alone decides.
No kernel may reach another device: no remote copies, remote signals or barrier semaphores. Data moves between devices by JAX's collectives and lax.ppermute only.
A program may use at most 128 MiB of HBM per device.

v0:
```python
import math
import jax
import jax.numpy as jnp
from jax import lax
from jax.sharding import PartitionSpec as P

PRECISE = lax.Precision.HIGHEST


def padded(value, sides, width, wrap):
    for axis, dim in sides:
        size, length = (lax.axis_size(axis), value.shape[dim])
        up = [(i, (i + 1) % size) for i in range(size if wrap else size - 1)]
        down = [(j, i) for i, j in up]
        last = lax.slice_in_dim(value, length - width, length, axis=dim)
        first = lax.slice_in_dim(value, 0, width, axis=dim)
        before = lax.ppermute(last, axis, up)
        after = lax.ppermute(first, axis, down)
        value = jnp.concatenate([before, value, after], axis=dim)
    return value


def face_flux(values, speeds, axis):
    count = values.shape[axis] - 2
    left_cells = lax.slice_in_dim(values, 0, count + 1, axis=axis)
    right_cells = lax.slice_in_dim(values, 1, count + 2, axis=axis)
    courant = lax.slice_in_dim(speeds, 0, count + 1, axis=axis)
    return 0.5 * courant * (left_cells + right_cells) - 0.5 * courant * courant * (
        right_cells - left_cells
    )


def real_basis(first_cell, count, length):
    cells = first_cell + jnp.arange(count, dtype=jnp.int32)
    column = jnp.arange(length, dtype=jnp.int32)
    half_length = length // 2
    frequency = jnp.where(column <= half_length, column, column - half_length)
    phase_index = cells[:, None] * frequency[None, :] % length
    angles = 2.0 * math.pi / length * phase_index.astype(jnp.float32)
    return jnp.where((column <= half_length)[None, :], jnp.cos(angles), jnp.sin(angles))


def column_factors(band_rows, length):
    column = jnp.arange(length, dtype=jnp.int32)
    half_length = length // 2
    frequency = jnp.where(column <= half_length, column, column - half_length)
    single = (column == 0) | (column == half_length)
    weights = jnp.where(single, 1.0 / length, 2.0 / length).astype(jnp.float32)
    ratios = (
        band_rows.astype(jnp.float32)[:, None]
        / jnp.maximum(frequency, 1).astype(jnp.float32)[None, :]
    )
    damping = jnp.minimum(1.0, ratios * ratios)
    return (damping - 1.0) * weights[None, :]


def polar_filter(values, band_rows):
    block_cells = values.shape[3]
    length = block_cells * lax.axis_size("lon")
    basis_table = real_basis(lax.axis_index("lon") * block_cells, block_cells, length)
    needed = jnp.any(band_rows < length // 2)

    def forward(grid):
        return jnp.einsum("flrn,nk->flrk", grid, basis_table, precision=PRECISE)

    def nothing(grid):
        return jnp.zeros(grid.shape[:3] + (length,), jnp.float32)

    partial_spec = lax.cond(needed, forward, nothing, values)
    spectrum = lax.psum(partial_spec, "lon")
    factors = column_factors(band_rows, length)

    def inverse(coeffs):
        return jnp.einsum(
            "flrk,nk->flrn", coeffs * factors[None, None], basis_table, precision=PRECISE
        )

    def no_change(coeffs):
        return jnp.zeros(coeffs.shape[:3] + (block_cells,), jnp.float32)

    return values + lax.cond(needed, inverse, no_change, spectrum)


def departure_terms(tracers, dep_owner, dep_row, dep_weight):
    band_count = lax.axis_size("lat")
    row_count, link_count = dep_owner.shape
    entries = row_count * link_count
    capacity = max(2, -(-2 * entries // band_count))
    owner_ids = dep_owner.reshape(entries)
    source = dep_row.reshape(entries)
    positions = jnp.arange(entries)
    earlier = (owner_ids[:, None] == owner_ids[None, :]) & (positions[None, :] < positions[:, None])
    slot_ids = jnp.sum(earlier.astype(jnp.int32), axis=1)
    band_ids = jnp.arange(band_count, dtype=jnp.int32)
    slot_range = jnp.arange(capacity, dtype=jnp.int32)
    matches = (owner_ids[:, None, None] == band_ids[None, :, None]) & (
        slot_ids[:, None, None] == slot_range[None, None, :]
    )
    request = jnp.sum(jnp.where(matches, source[:, None, None], 0), axis=0)
    wanted = lax.all_to_all(request, "lat", split_axis=0, concat_axis=0, tiled=True)
    by_row = jnp.transpose(tracers, (2, 0, 1, 3))
    outgoing = by_row[wanted]
    incoming = lax.all_to_all(outgoing, "lat", split_axis=0, concat_axis=0, tiled=True)
    stacked_rows = incoming.reshape((band_count * capacity,) + incoming.shape[2:])
    picked = stacked_rows[owner_ids * capacity + slot_ids].reshape(
        (row_count, link_count) + stacked_rows.shape[1:]
    )
    summed = dep_weight[:, 0][:, None, None, None] * picked[:, 0]
    summed = summed + dep_weight[:, 1][:, None, None, None] * picked[:, 1]
    return jnp.transpose(summed, (1, 2, 0, 3))


def body(
    prognostic,
    tracers,
    zonal_courant,
    meridional_courant,
    filter_band,
    dep_owner,
    dep_row,
    dep_weight,
):
    row_count = prognostic.shape[2]
    departed = departure_terms(tracers, dep_owner, dep_row, dep_weight)
    lon_padded = padded(
        jnp.concatenate([prognostic, zonal_courant[None]], axis=0), (("lon", 3),), 1, True
    )
    zonal_flux = face_flux(lon_padded[:-1], lon_padded[-1:], 3)
    lat_padded = padded(
        jnp.concatenate([prognostic, meridional_courant[None]], axis=0), (("lat", 2),), 1, False
    )
    merid_flux = face_flux(lat_padded[:-1], lat_padded[-1:], 2)
    total_rows = row_count * lax.axis_size("lat")
    face_rows = lax.axis_index("lat") * row_count + jnp.arange(row_count + 1) - 1
    merid_flux = jnp.where(
        (face_rows == total_rows - 1)[None, None, :, None], jnp.float32(0.0), merid_flux
    )
    advected = (
        prognostic
        - (zonal_flux[..., 1:] - zonal_flux[..., :-1])
        - (merid_flux[:, :, 1:] - merid_flux[:, :, :-1])
    )
    new_prognostic = polar_filter(advected, filter_band)
    return (new_prognostic, departed)


def solution(mesh):
    return jax.shard_map(
        body,
        mesh=mesh,
        in_specs=(
            P(None, None, "lat", "lon"),
            P(None, None, "lat", "lon"),
            P(None, "lat", "lon"),
            P(None, "lat", "lon"),
            P("lat"),
            P("lat", None),
            P("lat", None),
            P("lat", None),
        ),
        out_specs=(P(None, None, "lat", "lon"), P(None, None, "lat", "lon")),
        check_vma=False,
    )
```

profile of v0, /device:TPU:0, one launch (start us, length us, event | category | flops | bytes accessed | tf_op | source)
XLA Modules:
  0.0 461.9 jit_solution(5204649697896423825)
XLA Ops:
  7.2 0.8 copy.66
  7.9 0.1 eq.76
  8.0 0.2 convert_reduce_fusion
  8.2 0.8 copy.67
  9.0 0.1 broadcast_in_dim.68
  9.1 0.3 select_reduce_fusion
  9.4 0.7 copy.69
  10.1 7.3 %all-to-all-start = ((s32[8,1,12]{2,1,0:T(1,128)}), s32[8,1,12]{2,1,0:T(1,128)S(1)}, u32[]{:S(2)}, u32[]{:S(2)}) async-start(s32[8,1,12]{2,1,0:T(1,128)} %copy.69), calls=%async_computation | async-start | bytes 8192 | tf_op jit(solution)/shard_map/all_to_all | solution.py:100
  17.3 2.1 copy.83
  19.5 4.3 all-to-all-done
  23.7 0.1 reshape.169
  23.8 4.8 %gather_fusion = f32[96,4,16,384]{3,2,1,0:T(8,128)} fusion(f32[24,4,16,384]{3,2,1,0:T(8,128)S(1)} %bitcast.59, s32[1024]{0:T(1024)S(1)} %pad_clamp_fusion.1), kind=kCustom, calls=%fused_computation | custom fusion | bytes 18874752 | tf_op jit(solution)/shard_map/gather | solution.py:102
  28.6 5.3 %all-to-all-start.1 = ((f32[8,12,4,16,384]{4,3,2,1,0:T(8,128)}), f32[8,12,4,16,384]{4,3,2,1,0:T(8,128)}, u32[]{:S(2)}, u32[]{:S(2)}) async-start(f32[8,12,4,16,384]{4,3,2,1,0:T(8,128)} %bitcast.60), calls=%async_computation.1 | async-start | bytes 18874368 | tf_op jit(solution)/shard_map/all_to_all | solution.py:103
  33.9 0.0 copy-start.2
  34.0 0.0 all-reduce.2.cloned.1.call-start
  34.0 0.0 copy-done
  34.0 0.0 copy-done.4
  34.0 0.2 pad_maximum_fusion.11
  34.2 4.4 collective-permute-start.2
  38.6 0.7 copy.80
  39.3 1.3 collective-permute-start.3
  40.6 0.0 copy-start.9
  40.6 1.6 pad_maximum_fusion.8
  42.1 1.7 copy.77
  43.9 0.0 collective-permute-start
  43.9 1.7 copy.78
  45.6 1.8 collective-permute-start.1
  47.4 0.6 compare_reduce_fusion
  48.1 10.9 %sine_select_fusion = f32[384,1536]{1,0:T(8,128)} fusion(s32[1536]{0:T(1024)S(1)} %add_select_fusion.1, s32[384]{0:T(512)S(1)} %iota_add_fusion, pred[1536]{0:T(1024)(128)(4,1)S(1)} %iota_compare_fusion.2), kind=kLoop, calls=%fused_computation.42 | loop fusion | flops 5898240 | bytes 2368512 | tf_op jit(solution)/shard_map/jit(_where)/select_n | solution.py:40
  59.6 0.0 collective-permute-done
  59.6 0.5 copy.58
  60.1 0.0 collective-permute-done.1
  60.1 2.3 copy.60
  62.4 1.5 multiply_bitcast_fusion.1
  63.8 0.1 fusion.22
  64.0 0.0 copy-start.5
  64.0 1.5 multiply_subtract_fusion
  65.4 49.1 %collective-permute-done.2 = f32[5,16,1,384]{3,1,2,0:T(8,128)} collective-permute-done((f32[5,16,1,384]{3,1,2,0:T(8,128)S(1)}, f32[5,16,1,384]{3,1,2,0:T(8,128)}, u32[]{:S(2)}, u32[]{:S(2)}) %collective-permute-start.2) | collective-permute-done | bytes 122912 | tf_op jit(solution)/shard_map/ppermute | solution.py:17
  114.5 1.0 copy.62
  115.6 0.0 collective-permute-done.3
  115.6 1.0 copy.64
  116.6 0.2 multiply_bitcast_fusion
  116.8 0.1 fusion.23
  116.9 1.2 subtract_select_fusion
  118.0 2.3 fusion.16
  120.3 20.0 %conditional.2 = (f32[4,16,24,1536]{3,2,1,0:T(8,128)}) conditional(s32[]{:T(128)} %convert_element_type.23, () %tuple.57, (f32[4,16,24,384]{3,2,1,0:T(8,128)}, f32[384,1536]{1,0:T(8,128)}) %tuple.58), branch_computations={%region_1.2_spmd, %region_2.3_spmd} | conditional | flops 10871635968 | bytes 14155784 | solution.py:69
  120.3 20.0 %fusion = f32[4,16,24,1536]{3,2,1,0:T(8,128)} fusion(f32[4,16,24,384]{3,2,1,0:T(8,128)} %get-tuple-element.63, f32[384,1536]{1,0:T(8,128)} %get-tuple-element.64), kind=kOutput, calls=%fused_computation.2 | convolution fusion | flops 10871635968 | bytes 14155776 | tf_op jit(solution)/shard_map/cond/branch_1_fun/flrn,nk->flrk/dot_general | solution.py:64
  140.3 0.0 all-reduce.2.cloned.1.call-update
  140.3 0.6 copy-done.10
  140.9 0.0 copy-done.7
  141.0 0.1 copy.70
  141.1 0.1 mul.173
  141.2 0.0 copy-done.8
  141.2 278.5 %all-reduce.2.cloned.1.call-done = f32[4,16,24,1536]{3,2,1,0:T(8,128)} async-done(((f32[4,16,24,1536]{3,2,1,0:T(8,128)}), f32[4,16,24,1536]{3,2,1,0:T(8,128)}) %all-reduce.2.cloned.1.call-update) | async-done | bytes 9437200 | tf_op jit(solution)/shard_map/psum | solution.py:70
  419.8 0.0 copy-start.1
  419.8 19.6 %conditional.3 = (f32[4,16,24,384]{3,2,1,0:T(8,128)}) conditional(s32[]{:T(128)} %convert_element_type.23, () %tuple.56, (f32[24]{0:T(128)S(1)}, f32[1,1536]{1,0:T(1,128)S(1)}, s32[1,1536]{1,0:T(1,128)S(1)}, s32[1,1536]{1,0:T(1,128)S(1)}, f32[4,16,24,1536]{3,2,1,0:T(8,128)}, /*index=5*/f32[384,1536]{1,0:T(8,128)}) %tuple.59), branch_computations={%region_4.5_spmd, %region_5.6_spmd} | conditional | flops 10874185728 | bytes 14493804 | solution.py:81
  420.1 0.1 fusion.8
  420.2 19.2 %fusion.2 = f32[4,16,24,384]{3,2,1,0:T(8,128)} fusion(f32[4,16,24,1536]{3,2,1,0:T(8,128)} %get-tuple-element.65, f32[24,1536]{1,0:T(8,128)S(1)} %fusion.8, f32[384,1536]{1,0:T(8,128)} %get-tuple-element.70), kind=kOutput, calls=%fused_computation.4 | convolution fusion | flops 10873995264 | bytes 14303232 | tf_op jit(solution)/shard_map/cond/branch_1_fun/flrk,nk->flrn/dot_general | solution.py:74
  439.3 0.0 copy-done.1
  439.3 3.3 add.102
  442.6 0.0 all-to-all-done.1
  442.6 6.8 %gather_fusion.1 = f32[48,4,16,384]{3,2,1,0:T(8,128)} fusion(f32[96,4,16,384]{3,2,1,0:T(8,128)} %bitcast.15, s32[1024]{0:T(1024)S(1)} %pad_clamp_fusion), kind=kCustom, calls=%fused_computation.1 | custom fusion | bytes 9437376 | tf_op jit(solution)/shard_map/gather | solution.py:105
  449.4 2.9 fusion.14
  452.3 2.8 copy.72
  (31 shorter events, 0.2 us)
Async XLA Ops:
  10.1 13.7 %all-to-all-start = ((s32[8,1,12]{2,1,0:T(1,128)}), s32[8,1,12]{2,1,0:T(1,128)S(1)}, u32[]{:S(2)}, u32[]{:S(2)}) async-start(s32[8,1,12]{2,1,0:T(1,128)} %copy.69), calls=%async_computation | async-start | bytes 8192 | tf_op jit(solution)/shard_map/all_to_all | solution.py:100
  28.6 5.4 %copy-start = (f32[4,16,24,384]{3,2,1,0:T(8,128)S(1)}, f32[4,16,24,384]{3,2,1,0:T(8,128)}, u32[]{:S(2)}) copy-start(f32[4,16,24,384]{3,2,1,0:T(8,128)} %param.12) | copy-start | bytes 7077892
  28.6 5.4 %copy-start.4 = (f32[16,24,384]{2,1,0:T(8,128)S(1)}, f32[16,24,384]{2,1,0:T(8,128)}, u32[]{:S(2)}) copy-start(f32[16,24,384]{2,1,0:T(8,128)} %param.15) | copy-start | bytes 1769476
  28.6 414.0 %all-to-all-start.1 = ((f32[8,12,4,16,384]{4,3,2,1,0:T(8,128)}), f32[8,12,4,16,384]{4,3,2,1,0:T(8,128)}, u32[]{:S(2)}, u32[]{:S(2)}) async-start(f32[8,12,4,16,384]{4,3,2,1,0:T(8,128)} %bitcast.60), calls=%async_computation.1 | async-start | bytes 18874368 | tf_op jit(solution)/shard_map/all_to_all | solution.py:103
  33.9 6.6 %copy-start.2 = (f32[16,24,384]{2,1,0:T(8,128)S(1)}, f32[16,24,384]{2,1,0:T(8,128)}, u32[]{:S(2)}) copy-start(f32[16,24,384]{2,1,0:T(8,128)} %param.14) | copy-start | bytes 1769476
  34.0 385.8 %all-reduce.2.cloned.1.call-start = ((), (), s32[]{:S(2)}) async-start(), calls=%async_computation.2 | async-start | bytes 18874368 | tf_op jit(solution)/shard_map/psum | solution.py:70
  34.2 80.3 %collective-permute-start.2 = (f32[5,16,1,384]{3,1,2,0:T(8,128)S(1)}, f32[5,16,1,384]{3,1,2,0:T(8,128)}, u32[]{:S(2)}, u32[]{:S(2)}) collective-permute-start(f32[5,16,1,384]{3,1,2,0:T(8,128)S(1)} %copy.79), channel_id=1, source_target_pairs={{0,1},{1,2},{2,3},{3,4},{4,5},{5,6},{6,7},{8,9},{9,10},{10,11},{11... | collective-permute-start | bytes 368648 | tf_op jit(solution)/shard_map/ppermute | solution.py:17
  39.3 76.3 %collective-permute-start.3 = (f32[5,16,1,384]{3,1,2,0:T(8,128)}, f32[5,16,1,384]{3,1,2,0:T(8,128)}, u32[]{:S(2)}, u32[]{:S(2)}) collective-permute-start(f32[5,16,1,384]{3,1,2,0:T(8,128)} %copy.80), channel_id=1, source_target_pairs={{1,0},{2,1},{3,2},{4,3},{5,4},{6,5},{7,6},{9,8},{10,9},{11,10},{12... | collective-permute-start | bytes 368648 | tf_op jit(solution)/shard_map/ppermute | solution.py:18
  40.6 6.9 %copy-start.9 = (s32[24]{0:T(128)S(1)}, s32[24]{0:T(128)}, u32[]{:S(2)}) copy-start(s32[24]{0:T(128)} %param.16) | copy-start | bytes 292
  43.9 15.7 %collective-permute-start = (f32[5,16,24,1]{2,1,3,0:T(8,128)S(1)}, f32[5,16,24,1]{2,1,3,0:T(8,128)S(1)}, u32[]{:S(2)}, u32[]{:S(2)}) collective-permute-start(f32[5,16,24,1]{2,1,3,0:T(8,128)S(1)} %copy.77), channel_id=1, source_target_pairs={{0,8},{8,16},{16,24},{24,0},{1,9},{9,17},{17,25},{25,1},{2,10},{10... | collective-permute-start | bytes 23048 | tf_op jit(solution)/shard_map/ppermute | solution.py:17
  45.6 14.5 %collective-permute-start.1 = (f32[5,16,24,1]{2,1,3,0:T(8,128)S(1)}, f32[5,16,24,1]{2,1,3,0:T(8,128)}, u32[]{:S(2)}, u32[]{:S(2)}) collective-permute-start(f32[5,16,24,1]{2,1,3,0:T(8,128)S(1)} %copy.78), channel_id=1, source_target_pairs={{8,0},{16,8},{24,16},{0,24},{9,1},{17,9},{25,17},{1,25},{10,2},{18... | collective-permute-start | bytes 23048 | tf_op jit(solution)/shard_map/ppermute | solution.py:18
  62.4 1.6 copy-start.3
  62.4 1.6 copy-start.6
  64.0 52.6 %copy-start.5 = (f32[16,24,384]{2,1,0:T(8,128)S(1)}, f32[16,24,384]{2,1,0:T(8,128)}, u32[]{:S(2)}) copy-start(f32[16,24,384]{2,1,0:T(8,128)} %param.15) | copy-start | bytes 1769476
  140.3 0.7 copy-start.10
  140.3 0.7 copy-start.7
  140.3 0.9 copy-start.8
  419.8 19.6 %copy-start.1 = (f32[4,16,24,384]{3,2,1,0:T(8,128)S(1)}, f32[4,16,24,384]{3,2,1,0:T(8,128)}, u32[]{:S(2)}) copy-start(f32[4,16,24,384]{3,2,1,0:T(8,128)} %fusion.16) | copy-start | bytes 7077892
Sparse Core Ops, SparseCore 0:
  140.4 279.2 all-reduce.1
where the time goes:
time: 463 us; the launch traced here: 462 us
  waiting for transfers between devices  332 us (72%)
  matrix products  39.1 us (8%)
  local copies, waits for them, and re-layouts  28.8 us (6%)
  other arithmetic  26.8 us (6%)
  starting transfers between devices  20.1 us (4%)
  between operations  15 us (3%)
    psum x1, waiting for transfers between devices, polar_filter(): spectrum = lax.psum(partial_spec, 'lon')  279 us
    ppermute x2, waiting for transfers between devices, padded(): before = lax.ppermute(last, axis, up)  49.1 us
    dot_general x1, matrix products, forward(): return jnp.einsum('flrn,nk->flrk', grid, basis_table, precision=PRECISE)  20 us
    dot_general x1, matrix products, inverse(): jnp.einsum('flrk,nk->flrn', coeffs * factors[None, None], basis_table, pr...  19.2 us
    unnamed x30, local copies, waits for them, and re-layouts  11.2 us
    select_n x1, other arithmetic, real_basis(): jnp.where((column <= half_length)[None, :], jnp.cos(angles), jnp.sin(angl...  10.9 us
  transfers between devices with their start and end apart: 7, of which 3 were waited for; matrix products, arithmetic and copies ran while one was open for 16% of the time, Pallas kernels for 0%

commit v1 on v0

--- a/solution.py
+++ b/solution.py
@@ -67,7 +67,7 @@
         return jnp.zeros(grid.shape[:3] + (length,), jnp.float32)
 
     partial_spec = lax.cond(needed, forward, nothing, values)
-    spectrum = lax.psum(partial_spec, "lon")
+    spectrum = jnp.sum(lax.all_gather(partial_spec, "lon"), axis=0)
     factors = column_factors(band_rows, length)
 
     def inverse(coeffs):

time: 463 us -> 364 us (0.79)
  waiting for transfers between devices: 332 us -> 208 us
  other arithmetic: 26.8 us -> 50.3 us
    psum x1 -> x0, waiting for transfers between devices: 279 us -> none  [polar_filter(): spectrum = lax.psum(partial_spec, 'lon')]
    all_to_all x1, waiting for transfers between devices: 0.01 us -> 205 us  [departure_terms(): lax.all_to_all(outgoing, 'lat', split_axis=0, concat_axis=0, tiled=True)]
    ppermute x2, waiting for transfers between devices: 49.1 us -> 0.01 us  [padded(): before = lax.ppermute(last, axis, up)]
    reduce_sum x0 -> x1, other arithmetic: none -> 18.8 us  [polar_filter(): spectrum = jnp.sum(lax.all_gather(partial_spec, 'lon'), axis=0)]
    unnamed x30 -> x24, local copies, waits for them, and re-layouts: 11.2 us -> 10.4 us
  transfers between devices with their start and end apart: 7 -> 7, of which waited for: 3 -> 2; matrix products, arithmetic and copies ran while one was open for 16% -> 14% of each run, Pallas kernels for 0% -> 0%
where the time goes in v1:
time: 364 us; the launch traced here: 363 us
  waiting for transfers between devices  208 us (57%)
  other arithmetic  50.3 us (14%)
  matrix products  38.8 us (11%)
  local copies, waits for them, and re-layouts  29 us (8%)
  starting transfers between devices  21.4 us (6%)
  between operations  15 us (4%)
    all_to_all x1, waiting for transfers between devices, departure_terms(): lax.all_to_all(outgoing, 'lat', split_axis=0, concat_axis=0, tiled=True)  205 us
    dot_general x1, matrix products, forward(): return jnp.einsum('flrn,nk->flrk', grid, basis_table, precision=PRECISE)  19.8 us
    dot_general x1, matrix products, inverse(): jnp.einsum('flrk,nk->flrn', coeffs * factors[None, None], basis_table, pr...  19 us
    reduce_sum x1, other arithmetic, polar_filter(): spectrum = jnp.sum(lax.all_gather(partial_spec, 'lon'), axis=0)  18.8 us
    select_n x1, other arithmetic, real_basis(): jnp.where((column <= half_length)[None, :], jnp.cos(angles), jnp.sin(angl...  10.9 us
    unnamed x24, local copies, waits for them, and re-layouts  10.4 us
  transfers between devices with their start and end apart: 7, of which 2 were waited for; matrix products, arithmetic and copies ran while one was open for 14% of the time, Pallas kernels for 0%

profile of v1, /device:TPU:0, one launch (start us, length us, event | category | flops | bytes accessed | tf_op | source)
XLA Modules:
  0.0 362.8 jit_solution(14564308635350740693)
XLA Ops:
  7.2 0.0 copy-start
  7.2 0.0 copy-start.2
  7.2 0.0 all-gather.3.cloned.1.call-start
  7.2 1.9 pad_maximum_fusion.11
  9.1 0.7 copy.79
  9.8 5.5 %collective-permute-start.2 = (f32[5,16,1,384]{3,1,2,0:T(8,128)}, f32[5,16,1,384]{3,1,2,0:T(8,128)}, u32[]{:S(2)}, u32[]{:S(2)}) collective-permute-start(f32[5,16,1,384]{3,1,2,0:T(8,128)} %copy.79), channel_id=1, source_target_pairs={{0,1},{1,2},{2,3},{3,4},{4,5},{5,6},{6,7},{8,9},{9,10},{10,11},{11... | collective-permute-start | bytes 368648 | tf_op jit(solution)/shard_map/ppermute | solution.py:17
  15.3 1.3 collective-permute-start.3
  16.6 0.0 copy-done
  16.6 0.0 copy-done.2
  16.6 0.0 copy-start.7
  16.6 1.6 pad_maximum_fusion.8
  18.2 1.7 copy.77
  19.9 0.0 collective-permute-start
  20.0 1.7 copy.78
  21.7 1.8 collective-permute-start.1
  23.5 0.0 copy-done.7
  23.5 0.6 compare_reduce_fusion
  24.2 10.9 %sine_select_fusion = f32[384,1536]{1,0:T(8,128)} fusion(s32[1536]{0:T(1024)S(1)} %add_select_fusion.1, s32[384]{0:T(512)S(1)} %iota_add_fusion, pred[1536]{0:T(1024)(128)(4,1)S(1)} %iota_compare_fusion.2), kind=kLoop, calls=%fused_computation.42 | loop fusion | flops 5898240 | bytes 2368512 | tf_op jit(solution)/shard_map/jit(_where)/select_n | solution.py:40
  35.7 0.0 collective-permute-done
  35.7 1.3 copy.58
  37.0 2.2 multiply_bitcast_fusion.1
  39.2 1.0 fusion.22
  40.2 0.0 collective-permute-done.1
  40.2 1.5 copy.60
  41.7 2.7 multiply_subtract_fusion
  44.4 0.0 collective-permute-done.2
  44.4 1.0 copy.62
  45.5 0.0 copy-done.3
  45.5 0.2 multiply_bitcast_fusion
  45.7 0.1 fusion.23
  45.7 0.0 collective-permute-done.3
  45.8 1.0 copy.64
  46.8 1.2 subtract_select_fusion
  48.0 2.3 fusion.16
  50.2 19.8 %conditional.2 = (f32[4,16,24,1536]{3,2,1,0:T(8,128)}) conditional(s32[]{:T(128)} %convert_element_type.23, () %tuple.57, (f32[4,16,24,384]{3,2,1,0:T(8,128)}, f32[384,1536]{1,0:T(8,128)}) %tuple.58), branch_computations={%region_1.2_spmd, %region_2.3_spmd} | conditional | flops 10871635968 | bytes 14155784 | solution.py:69
  50.2 19.8 %fusion = f32[4,16,24,1536]{3,2,1,0:T(8,128)} fusion(f32[4,16,24,384]{3,2,1,0:T(8,128)} %get-tuple-element.67, f32[384,1536]{1,0:T(8,128)} %get-tuple-element.68), kind=kOutput, calls=%fused_computation.2 | convolution fusion | flops 10871635968 | bytes 14155776 | tf_op jit(solution)/shard_map/cond/branch_1_fun/flrn,nk->flrk/dot_general | solution.py:64
  70.1 0.0 all-gather.3.cloned.1.call-update
  70.1 0.7 copy-done.4
  70.8 0.1 copy.66
  70.8 0.1 eq.76
  70.9 0.0 copy-done.6
  70.9 0.1 copy.67
  71.0 0.1 broadcast_in_dim.68
  71.1 0.2 convert_reduce_fusion
  71.3 0.3 select_reduce_fusion
  71.6 0.7 copy.69
  72.3 6.9 %all-to-all-start = ((s32[8,1,12]{2,1,0:T(1,128)}), s32[8,1,12]{2,1,0:T(1,128)S(1)}, u32[]{:S(2)}, u32[]{:S(2)}) async-start(s32[8,1,12]{2,1,0:T(1,128)} %copy.69), calls=%async_computation | async-start | bytes 8192 | tf_op jit(solution)/shard_map/all_to_all | solution.py:100
  79.2 2.7 copy.83
  81.9 3.7 %all-to-all-done = s32[8,1,12]{2,1,0:T(1,128)S(1)} async-done(((s32[8,1,12]{2,1,0:T(1,128)}), s32[8,1,12]{2,1,0:T(1,128)S(1)}, u32[]{:S(2)}, u32[]{:S(2)}) %all-to-all-start) | async-done | bytes 416 | tf_op jit(solution)/shard_map/all_to_all | solution.py:100
  85.6 0.1 reshape.169
  85.7 6.0 %gather_fusion = f32[96,4,16,384]{3,2,1,0:T(8,128)} fusion(f32[24,4,16,384]{3,2,1,0:T(8,128)S(1)} %bitcast.60, s32[1024]{0:T(1024)S(1)} %pad_clamp_fusion.1), kind=kCustom, calls=%fused_computation | custom fusion | bytes 18874752 | tf_op jit(solution)/shard_map/gather | solution.py:102
  91.7 5.8 %all-to-all-start.1 = ((f32[8,12,4,16,384]{4,3,2,1,0:T(8,128)}), f32[8,12,4,16,384]{4,3,2,1,0:T(8,128)}, u32[]{:S(2)}, u32[]{:S(2)}) async-start(f32[8,12,4,16,384]{4,3,2,1,0:T(8,128)} %bitcast.61), calls=%async_computation.1 | async-start | bytes 18874368 | tf_op jit(solution)/shard_map/all_to_all | solution.py:103
  97.5 0.1 copy.70
  97.6 0.1 mul.173
  97.8 204.6 %all-to-all-done.1 = f32[8,12,4,16,384]{4,3,2,1,0:T(8,128)} async-done(((f32[8,12,4,16,384]{4,3,2,1,0:T(8,128)}), f32[8,12,4,16,384]{4,3,2,1,0:T(8,128)}, u32[]{:S(2)}, u32[]{:S(2)}) %all-to-all-start.1) | async-done | bytes 9437216 | tf_op jit(solution)/shard_map/all_to_all | solution.py:103
  302.4 6.6 %gather_fusion.1 = f32[48,4,16,384]{3,2,1,0:T(8,128)} fusion(f32[96,4,16,384]{3,2,1,0:T(8,128)} %bitcast.16, s32[1024]{0:T(1024)S(1)} %pad_clamp_fusion), kind=kCustom, calls=%fused_computation.1 | custom fusion | bytes 9437376 | tf_op jit(solution)/shard_map/gather | solution.py:105
  309.0 2.9 fusion.14
  311.9 2.8 copy.72
  314.7 0.0 copy-start.1
  314.7 37.9 %conditional.3 = (f32[4,16,24,384]{3,2,1,0:T(8,128)}) conditional(s32[]{:T(128)} %convert_element_type.23, () %tuple.56, (f32[4,4,16,24,1536]{4,3,2,1,0:T(8,128)}, f32[24]{0:T(128)S(1)}, f32[1,1536]{1,0:T(1,128)S(1)}, s32[1,1536]{1,0:T(1,128)S(1)}, s32[1,1536]{1,0:T(1,128)S(1)}, /*index=5*/f32[384,1536]{1,0:T(8,128)}) %tuple.77), branch_computations={%region_3.4_spmd, %region_4.6_spmd} | conditional | flops 10881263616 | bytes 61679728 | solution.py:81
  314.7 18.8 %reduce_sum.27 = f32[4,16,24,1536]{3,2,1,0:T(8,128)} reduce(f32[4,4,16,24,1536]{4,3,2,1,0:T(8,128)} %get-tuple-element.69, f32[]{:T(128)} %constant.26.clone), dimensions={0}, to_apply=%region_5.5 | reduce | flops 7077888 | bytes 47185924 | tf_op jit(solution)/shard_map/reduce_sum | solution.py:70
  333.6 0.1 fusion.8
  333.7 19.0 %fusion.2 = f32[4,16,24,384]{3,2,1,0:T(8,128)} fusion(f32[4,16,24,1536]{3,2,1,0:T(8,128)} %reduce_sum.27, f32[24,1536]{1,0:T(8,128)S(1)} %fusion.8, f32[384,1536]{1,0:T(8,128)} %get-tuple-element.74), kind=kOutput, calls=%fused_computation.4 | convolution fusion | flops 10873995264 | bytes 14303232 | tf_op jit(solution)/shard_map/cond/branch_1_fun/flrk,nk->flrn/dot_general | solution.py:74
  352.6 3.3 add.100
  (26 shorter events, 0.2 us)
Async XLA Ops:
  7.2 9.5 %copy-start = (f32[4,16,24,384]{3,2,1,0:T(8,128)S(1)}, f32[4,16,24,384]{3,2,1,0:T(8,128)}, u32[]{:S(2)}) copy-start(f32[4,16,24,384]{3,2,1,0:T(8,128)} %param.12) | copy-start | bytes 7077892
  7.2 9.5 %copy-start.2 = (f32[16,24,384]{2,1,0:T(8,128)S(1)}, f32[16,24,384]{2,1,0:T(8,128)}, u32[]{:S(2)}) copy-start(f32[16,24,384]{2,1,0:T(8,128)} %param.14) | copy-start | bytes 1769476
  7.2 307.5 %all-gather.3.cloned.1.call-start = ((), (), s32[]{:S(2)}) async-start(), calls=%async_computation.2 | async-start | bytes 47185920 | tf_op jit(solution)/shard_map/all_gather | solution.py:70
  9.8 34.6 %collective-permute-start.2 = (f32[5,16,1,384]{3,1,2,0:T(8,128)}, f32[5,16,1,384]{3,1,2,0:T(8,128)}, u32[]{:S(2)}, u32[]{:S(2)}) collective-permute-start(f32[5,16,1,384]{3,1,2,0:T(8,128)} %copy.79), channel_id=1, source_target_pairs={{0,1},{1,2},{2,3},{3,4},{4,5},{5,6},{6,7},{8,9},{9,10},{10,11},{11... | collective-permute-start | bytes 368648 | tf_op jit(solution)/shard_map/ppermute | solution.py:17
  15.3 30.4 %collective-permute-start.3 = (f32[5,16,1,384]{3,1,2,0:T(8,128)S(1)}, f32[5,16,1,384]{3,1,2,0:T(8,128)}, u32[]{:S(2)}, u32[]{:S(2)}) collective-permute-start(f32[5,16,1,384]{3,1,2,0:T(8,128)S(1)} %copy.80), channel_id=1, source_target_pairs={{1,0},{2,1},{3,2},{4,3},{5,4},{6,5},{7,6},{9,8},{10,9},{11,10},{12... | collective-permute-start | bytes 368648 | tf_op jit(solution)/shard_map/ppermute | solution.py:18
  16.6 6.9 %copy-start.7 = (s32[24]{0:T(128)S(1)}, s32[24]{0:T(128)}, u32[]{:S(2)}) copy-start(s32[24]{0:T(128)} %param.16) | copy-start | bytes 292
  19.9 15.7 %collective-permute-start = (f32[5,16,24,1]{2,1,3,0:T(8,128)S(1)}, f32[5,16,24,1]{2,1,3,0:T(8,128)}, u32[]{:S(2)}, u32[]{:S(2)}) collective-permute-start(f32[5,16,24,1]{2,1,3,0:T(8,128)S(1)} %copy.77), channel_id=1, source_target_pairs={{0,8},{8,16},{16,24},{24,0},{1,9},{9,17},{17,25},{25,1},{2,10},{10... | collective-permute-start | bytes 23048 | tf_op jit(solution)/shard_map/ppermute | solution.py:17
  21.7 18.5 %collective-permute-start.1 = (f32[5,16,24,1]{2,1,3,0:T(8,128)S(1)}, f32[5,16,24,1]{2,1,3,0:T(8,128)S(1)}, u32[]{:S(2)}, u32[]{:S(2)}) collective-permute-start(f32[5,16,24,1]{2,1,3,0:T(8,128)S(1)} %copy.78), channel_id=1, source_target_pairs={{8,0},{16,8},{24,16},{0,24},{9,1},{17,9},{25,17},{1,25},{10,2},{18... | collective-permute-start | bytes 23048 | tf_op jit(solution)/shard_map/ppermute | solution.py:18
  41.7 3.8 %copy-start.3 = (f32[16,24,384]{2,1,0:T(8,128)S(1)}, f32[16,24,384]{2,1,0:T(8,128)}, u32[]{:S(2)}) copy-start(f32[16,24,384]{2,1,0:T(8,128)} %param.15) | copy-start | bytes 1769476
  70.1 0.7 copy-start.4
  70.1 0.9 copy-start.6
  72.3 13.3 %all-to-all-start = ((s32[8,1,12]{2,1,0:T(1,128)}), s32[8,1,12]{2,1,0:T(1,128)S(1)}, u32[]{:S(2)}, u32[]{:S(2)}) async-start(s32[8,1,12]{2,1,0:T(1,128)} %copy.69), calls=%async_computation | async-start | bytes 8192 | tf_op jit(solution)/shard_map/all_to_all | solution.py:100
  91.7 6.0 %copy-start.5 = (f32[24,2]{0,1:T(2,128)S(1)}, f32[24,2]{0,1:T(2,128)}, u32[]{:S(2)}) copy-start(f32[24,2]{0,1:T(2,128)} %param.19) | copy-start | bytes 580
  91.7 210.6 %all-to-all-start.1 = ((f32[8,12,4,16,384]{4,3,2,1,0:T(8,128)}), f32[8,12,4,16,384]{4,3,2,1,0:T(8,128)}, u32[]{:S(2)}, u32[]{:S(2)}) async-start(f32[8,12,4,16,384]{4,3,2,1,0:T(8,128)} %bitcast.61), calls=%async_computation.1 | async-start | bytes 18874368 | tf_op jit(solution)/shard_map/all_to_all | solution.py:103
  314.7 37.9 %copy-start.1 = (f32[4,16,24,384]{3,2,1,0:T(8,128)S(1)}, f32[4,16,24,384]{3,2,1,0:T(8,128)}, u32[]{:S(2)}) copy-start(f32[4,16,24,384]{3,2,1,0:T(8,128)} %fusion.16) | copy-start | bytes 7077892
Sparse Core Ops, SparseCore 0:
  70.2 229.5 all-gather.2
